TPU v7x, 256 devices: a whole 4x4x8 slice. The times are simulated.
256 devices in a mesh: seq: 32 (over y, x, core), dev: 8 (over z).
Axes of the slice: x: 4, y: 4, z: 8, core: 2. Of those that a mesh axis runs over, the one named last changes fastest.
Arguments:
- queries: bfloat16 [2048, 4096], P('seq', 'dev'), may hold values from -6 to 6
- key_vectors: bfloat16 [2048, 4096], P('seq', 'dev'), may hold values from -6 to 6
- value_vectors: bfloat16 [2048, 4096], P('seq', 'dev'), may hold values from -6 to 6
- log_decay: float32 [2048, 32], P('seq', 'dev')
- head_gain: float32 [4096], P('dev'), may hold values from 0.5 to 1.5
- gate_weight: bfloat16 [8, 4096, 4096], P('dev', None, 'seq'), may hold values from -0.09375 to 0.09375
- up_weight: bfloat16 [8, 4096, 4096], P('dev', None, 'seq'), may hold values from -0.09375 to 0.09375
- down_weight: bfloat16 [8, 4096, 4096], P('dev', 'seq'), may hold values from -0.0625 to 0.0625
- expert_ids: int32 [2048, 2], P(('seq', 'dev')), may hold values from 0 to 3, all different within a row; in each aligned block of 8 rows (0 to 7, 8 to 15, ...) at most 6 rows name the same one
- expert_weights: float32 [2048, 2], P(('seq', 'dev')), may hold values from 0.2 to 1
Outputs:
- layer_output: bfloat16 [2048, 4096], P(('seq', 'dev'))
Inputs may be any that keep to these rules, and one draw needn't show every extreme that they name: `expert_ids`: in each aligned block of 8 rows (the tokens of one device) no expert is named by more than 6 rows, a bound that some block reaches; the two experts of a row differ.
All inputs are finite; a program needn't handle non-finite values.
Results may differ from a plain program's by a relative error of at most 0.03.
Values may be sent and summed in bfloat16 or wider, within the bound.
No kernel may reach another device: no remote copies, remote signals or barrier semaphores. Data moves between devices by JAX's collectives and lax.ppermute only.
A program may use at most 128 MiB of HBM per device.

v0:
```python
import jax
import jax.numpy as jnp
from jax import lax
from jax.sharding import PartitionSpec as P

PAIR = 2
BLOCK_MAX = 512
highest = lax.Precision.HIGHEST


def carried_in(value, axis, join, neutral):
    place = lax.axis_index(axis)
    gathered = jax.tree.map(
        lambda a, kind: lax.all_gather(a.astype(kind), axis), value, (jnp.bfloat16, jnp.bfloat16)
    )
    state = jax.tree.map(lambda a, e: jnp.zeros_like(a) + jnp.asarray(e, a.dtype), value, neutral)

    def one(turn, state):
        return join(
            state,
            jax.tree.map(
                lambda a, own: lax.dynamic_index_in_dim(a, turn, 0, False).astype(own.dtype),
                gathered,
                value,
            ),
        )

    return lax.fori_loop(0, place, one, state)


def block_step(state, pieces):
    queries_blk, keys_blk, values_blk, decay_blk = pieces
    length = decay_blk.shape[0]
    running = jnp.cumsum(decay_blk)
    causal = jnp.arange(length)[:, None] >= jnp.arange(length)[None, :]
    spread = jnp.where(causal, running[:, None] - running[None, :], 0.0)
    factors = jnp.where(causal, jnp.exp(spread), 0.0)
    scores = jnp.dot(queries_blk, keys_blk.T, preferred_element_type=jnp.float32) * factors
    values_f = values_blk.astype(jnp.float32)
    keys_f = keys_blk.astype(jnp.float32)
    carried = jnp.exp(running)[:, None] * jnp.dot(
        queries_blk.astype(jnp.float32), state, precision=highest
    )
    output = jnp.dot(scores, values_f, precision=highest) + carried
    tail_decay = jnp.exp(running[-1] - running)
    state = jnp.exp(running[-1]) * state + jnp.dot(
        (keys_f * tail_decay[:, None]).T, values_f, precision=highest
    )
    return (state, output)


def run_blocks(state, queries_b, keys_b, values_b, decay_f, block):
    count = decay_f.shape[0] // block
    shaped = (
        queries_b.reshape(count, block, -1),
        keys_b.reshape(count, block, -1),
        values_b.reshape(count, block, -1),
        decay_f.reshape(count, block),
    )
    state, outputs = lax.scan(block_step, state, shaped)
    return outputs.reshape(count * block, -1)


def head_norm(attention, gain):
    square_mean = jnp.mean(attention * attention, axis=-1, keepdims=True)
    return (attention * lax.rsqrt(square_mean + 1e-06) * gain).astype(jnp.bfloat16)


def slot_ranks(flat_experts, experts):
    onehot = (flat_experts[..., None] == jnp.arange(experts, dtype=jnp.int32)).astype(jnp.int32)
    before = jnp.cumsum(onehot, axis=-2) - onehot
    return jnp.sum(before * onehot, axis=-1)


def chain_join(earlier, later):
    return (earlier[0] + later[0], jnp.exp(later[0])[:, None, None] * earlier[1] + later[1])


def per_device(
    queries,
    key_vectors,
    value_vectors,
    log_decay,
    head_gain,
    gate_weight,
    up_weight,
    down_weight,
    expert_ids,
    expert_weights,
):
    seq_len = queries.shape[0]
    heads = log_decay.shape[1]
    head_dim = queries.shape[1] // heads
    queries_h = jnp.transpose(queries.reshape(seq_len, heads, head_dim), (1, 0, 2))
    keys_h = jnp.transpose(key_vectors.reshape(seq_len, heads, head_dim), (1, 0, 2))
    values_h = jnp.transpose(value_vectors.reshape(seq_len, heads, head_dim), (1, 0, 2))
    decay_h = jnp.transpose(log_decay, (1, 0))
    running = jnp.cumsum(decay_h, axis=1)
    log_total = running[:, -1]
    tail_decay = jnp.exp(log_total[:, None] - running)
    local_state = jnp.einsum(
        "hsa,hsb->hab",
        keys_h.astype(jnp.float32) * tail_decay[:, :, None],
        values_h.astype(jnp.float32),
        precision=highest,
    )
    starting = (jnp.zeros((heads,), jnp.float32), jnp.zeros_like(local_state))
    incoming = carried_in((log_total, local_state), "seq", chain_join, starting)[1]
    block = min(BLOCK_MAX, seq_len)

    def one_head(state, head_queries, head_keys, head_values, head_decay):
        return run_blocks(state, head_queries, head_keys, head_values, head_decay, block)

    attention = jax.vmap(one_head)(incoming, queries_h, keys_h, values_h, decay_h)
    normed_h = head_norm(attention, head_gain.reshape(heads, 1, head_dim))
    normed = jnp.transpose(normed_h, (1, 0, 2)).reshape(seq_len, heads * head_dim)
    dev_count = lax.axis_size("dev")
    experts = dev_count // PAIR
    tok_count = expert_ids.shape[0]
    top_count = expert_ids.shape[1]
    capacity = max(2, (3 * tok_count * top_count + 2 * experts - 1) // (2 * experts))
    head_size = normed.shape[1]
    width = head_size * dev_count
    own_flat = expert_ids.reshape(tok_count * top_count)
    own_rank = slot_ranks(own_flat[None, :], experts)[0]
    pick_index = own_flat * capacity + own_rank
    owned_rows = lax.all_to_all(normed, "dev", split_axis=0, concat_axis=1, tiled=True)
    slot_token = (
        jnp.full((experts * capacity,), tok_count, jnp.int32)
        .at[pick_index]
        .set(jnp.arange(tok_count * top_count, dtype=jnp.int32) // top_count)
    )
    padded = jnp.concatenate([owned_rows, jnp.zeros((1, width), owned_rows.dtype)], axis=0)
    send_rows = jnp.repeat(padded[slot_token].reshape(experts, capacity, width), PAIR, axis=0)
    arrived = lax.all_to_all(send_rows, "dev", split_axis=0, concat_axis=0, tiled=True)
    local_rows = arrived.reshape(-1, width)
    piece = lax.all_gather(local_rows, "seq", axis=0, tiled=True)
    gate_part = jnp.dot(piece, gate_weight[0], preferred_element_type=jnp.float32)
    up_part = jnp.dot(piece, up_weight[0], preferred_element_type=jnp.float32)
    hidden_all = (jax.nn.silu(gate_part) * up_part).astype(jnp.bfloat16)
    piece = hidden_all
    term = jnp.dot(piece, down_weight[0], preferred_element_type=jnp.float32).astype(jnp.bfloat16)
    term = lax.optimization_barrier(term)
    summed = lax.psum_scatter(
        term.astype(jnp.float32).astype(jnp.bfloat16), "seq", scatter_dimension=0, tiled=True
    ).astype(jnp.float32)
    returned = lax.all_to_all(
        summed.reshape(dev_count, capacity, width).astype(jnp.bfloat16),
        "dev",
        split_axis=0,
        concat_axis=0,
        tiled=True,
    ).astype(jnp.float32)
    expert_out = jnp.sum(returned.reshape(experts, PAIR, capacity, width), axis=1).astype(
        jnp.bfloat16
    )
    picked = expert_out.reshape(experts * capacity, width)[pick_index].reshape(
        tok_count, top_count, width
    )
    combined = jnp.sum(picked.astype(jnp.float32) * expert_weights[:, :, None], axis=1)
    return combined.astype(jnp.bfloat16)


def solution(mesh):
    in_specs = (
        P("seq", "dev"),
        P("seq", "dev"),
        P("seq", "dev"),
        P("seq", "dev"),
        P("dev"),
        P("dev", None, "seq"),
        P("dev", None, "seq"),
        P("dev", "seq", None),
        P(("seq", "dev"), None),
        P(("seq", "dev"), None),
    )
    out_specs = P(("seq", "dev"), None)
    return jax.shard_map(
        per_device, mesh=mesh, in_specs=in_specs, out_specs=out_specs, check_vma=False
    )
```

profile of v0, /device:TPU:2, one launch (start us, length us, event | category | flops | bytes accessed | tf_op | source)
XLA Modules:
  0.0 384.8 jit_solution(10453502567396986454)
XLA Ops:
  6.5 0.0 copy-start
  6.5 0.0 all-gather.7.cloned.1.call-start
  6.5 1.0 reduce_window_sum.25
  7.5 0.2 slice_reduce_fusion
  7.7 0.1 exponential_bitcast_fusion.1
  7.8 2.0 convolution_convert_fusion.1
  9.8 0.0 all-gather.7.cloned.1.call-update
  9.8 1.3 dynamic-slice.8
  11.7 0.2 fusion.30
  11.9 0.2 dynamic-update-slice
  12.2 62.8 %all-reduce.1 = bf16[128]{0:T(256)(128)(2,1)S(1)} all-reduce(bf16[128]{0:T(256)(128)(2,1)S(1)} %dynamic-update-slice), channel_id=2, replica_groups=mesh['seq'=32,'dev'=8] {'seq'}, use_global_device_ids=true, to_apply=%add.1 | all-reduce | flops 128 | bytes 512
  75.0 0.1 reshape.263
  75.1 0.8 copy.29
  75.9 0.1 eq.27
  75.9 0.1 fusion.29
  76.0 0.7 broadcast_multiply_fusion
  76.7 0.1 copy.28
  76.8 0.1 mul.129
  76.9 0.2 select_reduce_fusion
  77.1 0.6 scatter_custom_fusion
  77.7 1.0 convolution_multiply_fusion.1
  78.8 0.0 all-gather.7.cloned.1.call-done
  78.8 0.0 copy-start.1
  78.8 2.2 while.3
  78.9 1.1 convert_add_fusion.2
  80.0 1.0 convert_add_fusion.2
  81.1 1.1 fusion.21
  82.2 1.1 fusion.13
  83.3 0.8 fusion.17
  84.1 0.1 copy.27
  84.2 0.7 all_to_all.20
  84.9 8.2 %all-to-all-start = ((bf16[8,8,512]{2,1,0:T(8,128)(2,1)}), bf16[8,8,512]{2,1,0:T(8,128)(2,1)S(1)}, u32[]{:S(2)}, u32[]{:S(2)}) async-start(bf16[8,8,512]{2,1,0:T(8,128)(2,1)} %all_to_all.20), calls=%async_computation | async-start | bytes 131072 | tf_op jit(solution)/shard_map/all_to_all | solution.py:127
  93.1 0.0 all-gather.5.cloned.1.call-start
  93.1 8.3 %all-to-all-done = bf16[8,8,512]{2,1,0:T(8,128)(2,1)S(1)} async-done(((bf16[8,8,512]{2,1,0:T(8,128)(2,1)}), bf16[8,8,512]{2,1,0:T(8,128)(2,1)S(1)}, u32[]{:S(2)}, u32[]{:S(2)}) %all-to-all-start) | async-done | bytes 65568 | tf_op jit(solution)/shard_map/all_to_all | solution.py:127
  101.4 0.7 gather_fusion
  102.1 0.1 reshape.232
  102.2 15.7 %all_to_all.29 = bf16[8,6,4096]{2,1,0:T(8,128)(2,1)S(1)} all-to-all(bf16[8,6,4096]{2,1,0:T(8,128)(2,1)S(1)} %bitcast.114), channel_id=1, replica_groups=mesh['seq'=32,'dev'=8] {'dev'}, dimensions={0} | all-to-all | bytes 786432 | tf_op jit(solution)/shard_map/all_to_all | solution.py:135
  117.9 0.9 reshape.234
  118.9 0.0 all-gather.5.cloned.1.call-update
  118.9 0.0 reduce-scatter.2.cloned.1.call-start
  118.9 95.2 %all-gather.5.cloned.1.call-done = bf16[1536,4096]{1,0:T(8,128)(2,1)} async-done(((bf16[48,4096]{1,0:T(8,128)(2,1)}), bf16[1536,4096]{1,0:T(8,128)(2,1)}) %all-gather.5.cloned.1.call-update) | async-done | bytes 12582928 | tf_op jit(solution)/shard_map/all_gather | solution.py:137
  214.2 6.7 %fusion.4 = f32[1536,128]{1,0:T(8,128)S(1)} fusion(bf16[1536,4096]{1,0:T(8,128)(2,1)} %all-gather.5.cloned.1.call-done, bf16[1,4096,128]{2,1,0:T(8,128)(2,1)} %param.17), kind=kOutput, calls=%fused_computation.12 | convolution fusion | flops 1610612736 | bytes 14417920 | tf_op jit(solution)/shard_map/dot_general | solution.py:138
  220.9 0.0 copy-done
  220.9 0.0 copy-done.1
  220.9 18.6 %convolution_convert_fusion = bf16[1536,4096]{1,0:T(8,128)(2,1)} fusion(bf16[1536,4096]{1,0:T(8,128)(2,1)} %all-gather.5.cloned.1.call-done, bf16[1,128,4096]{2,1,0:T(8,128)(2,1)S(1)} %copy-done, bf16[1,4096,128]{2,1,0:T(8,128)(2,1)S(1)} %copy-done.1, f32[1536,128]{1,0:T(8,128)S(1)} %fusion.4), kind=kOutput, calls=%fused_computation.5 | convolution fusion | flops 3228696576 | bytes 28049408 | tf_op jit(solution)/shard_map/dot_general | solution.py:142
  239.5 0.0 copy-start.2
  239.5 0.0 reduce-scatter.2.cloned.1.call-update
  239.5 111.4 %reduce-scatter.2.cloned.1.call-done = bf16[48,4096]{1,0:T(8,128)(2,1)} async-done(((bf16[1536,4096]{1,0:T(8,128)(2,1)}), bf16[48,4096]{1,0:T(8,128)(2,1)}) %reduce-scatter.2.cloned.1.call-update) | async-done | bytes 393232 | tf_op jit(solution)/shard_map/reduce_scatter | solution.py:144
  350.9 1.9 convert_element_type.99
  352.8 7.0 %all-to-all-start.2 = ((bf16[8,6,4096]{2,1,0:T(8,128)(2,1)}), bf16[8,6,4096]{2,1,0:T(8,128)(2,1)S(1)}, u32[]{:S(2)}, u32[]{:S(2)}) async-start(bf16[8,6,4096]{2,1,0:T(8,128)(2,1)} %convert_element_type.99), calls=%async_computation.3 | async-start | bytes 1048576 | tf_op jit(solution)/shard_map/all_to_all | solution.py:147
  359.9 0.0 copy-done.2
  359.9 0.1 copy.30
  360.0 16.3 %all-to-all-done.2 = bf16[8,6,4096]{2,1,0:T(8,128)(2,1)S(1)} async-done(((bf16[8,6,4096]{2,1,0:T(8,128)(2,1)}), bf16[8,6,4096]{2,1,0:T(8,128)(2,1)S(1)}, u32[]{:S(2)}, u32[]{:S(2)}) %all-to-all-start.2) | async-done | bytes 393248 | tf_op jit(solution)/shard_map/all_to_all | solution.py:147
  376.3 0.1 bitcast_reduce_fusion
  376.4 0.1 convert_element_type.101
  376.5 0.6 gather_fusion.1
  377.1 0.2 reshape.238
  377.3 1.0 multiply_reduce_fusion
  (14 shorter events, 0.2 us)
Async XLA Ops:
  6.5 214.3 %copy-start = (bf16[1,128,4096]{2,1,0:T(8,128)(2,1)S(1)}, bf16[1,128,4096]{2,1,0:T(8,128)(2,1)}, u32[]{:S(2)}) copy-start(bf16[1,128,4096]{2,1,0:T(8,128)(2,1)} %param.19) | copy-start | bytes 3145732
  6.5 72.3 %all-gather.7.cloned.1.call-start = ((), (), s32[]{:S(2)}) async-start(), calls=%async_computation.6 | async-start | bytes 4325376 | tf_op jit(solution)/shard_map/all_gather | solution.py:14
  78.8 142.0 %copy-start.1 = (bf16[1,4096,128]{2,1,0:T(8,128)(2,1)S(1)}, bf16[1,4096,128]{2,1,0:T(8,128)(2,1)}, u32[]{:S(2)}) copy-start(bf16[1,4096,128]{2,1,0:T(8,128)(2,1)} %param.18) | copy-start | bytes 3145732
  84.9 16.6 %all-to-all-start = ((bf16[8,8,512]{2,1,0:T(8,128)(2,1)}), bf16[8,8,512]{2,1,0:T(8,128)(2,1)S(1)}, u32[]{:S(2)}, u32[]{:S(2)}) async-start(bf16[8,8,512]{2,1,0:T(8,128)(2,1)} %all_to_all.20), calls=%async_computation | async-start | bytes 131072 | tf_op jit(solution)/shard_map/all_to_all | solution.py:127
  93.1 121.1 %all-gather.5.cloned.1.call-start = ((), (), s32[]{:S(2)}) async-start(), calls=%async_computation.4 | async-start | bytes 12976128 | tf_op jit(solution)/shard_map/all_gather | solution.py:137
  118.9 232.0 %reduce-scatter.2.cloned.1.call-start = ((), (), s32[]{:S(2)}) async-start(), calls=%async_computation.5 | async-start | bytes 12976128 | tf_op jit(solution)/shard_map/reduce_scatter | solution.py:144
  239.5 120.4 %copy-start.2 = (f32[8,2]{0,1:T(2,128)S(1)}, f32[8,2]{0,1:T(2,128)}, u32[]{:S(2)}) copy-start(f32[8,2]{0,1:T(2,128)} %param.21) | copy-start | bytes 196
  352.8 23.4 %all-to-all-start.2 = ((bf16[8,6,4096]{2,1,0:T(8,128)(2,1)}), bf16[8,6,4096]{2,1,0:T(8,128)(2,1)S(1)}, u32[]{:S(2)}, u32[]{:S(2)}) async-start(bf16[8,6,4096]{2,1,0:T(8,128)(2,1)} %convert_element_type.99), calls=%async_computation.3 | async-start | bytes 1048576 | tf_op jit(solution)/shard_map/all_to_all | solution.py:147
Sparse Core Ops, SparseCore 0:
  9.9 53.7 all-gather.6
  119.0 95.1 all-gather.4
  239.6 111.2 reduce-scatter.1
where the time goes:
time: 386 us; the launch traced here: 385 us
  waiting for transfers between devices  231 us (60%)
  blocking collectives  78.5 us (20%)
  matrix products  30.5 us (8%)
  starting transfers between devices  15.3 us (4%)
  between operations  14 us (4%)
  local copies, waits for them, and re-layouts  8.93 us (2%)
  other arithmetic  6.19 us (2%)
    reduce_scatter x1, waiting for transfers between devices, per_device(): lax.psum_scatter(term.astype(jnp.float32).astype(jnp.bfloat16), 'seq', sc...  111 us
    all_gather x1, waiting for transfers between devices, per_device(): piece = lax.all_gather(local_rows, 'seq', axis=0, tiled=True)  95.2 us
    unnamed x1, blocking collectives  62.8 us
    dot_general x1, matrix products, per_device(): jnp.dot(piece, down_weight[0], preferred_element_type=jnp.float32)  18.6 us
    all_to_all x1, waiting for transfers between devices, per_device(): lax.all_to_all(summed.reshape(dev_count, capacity, width).astype(jnp.bflo...  16.3 us
    all_to_all x1, blocking collectives, per_device(): lax.all_to_all(send_rows, 'dev', split_axis=0, concat_axis=0, tiled=True)  15.7 us
    all_to_all x1, waiting for transfers between devices, per_device(): lax.all_to_all(normed, 'dev', split_axis=0, concat_axis=1, tiled=True)  8.31 us
    all_to_all x1, starting transfers between devices, per_device(): lax.all_to_all(normed, 'dev', split_axis=0, concat_axis=1, tiled=True)  8.19 us
  transfers between devices with their start and end apart: 5, of which 4 were waited for; matrix products, arithmetic and copies ran while one was open for 1% of the time, Pallas kernels for 0%

commit v1 on v0

--- a/solution.py
+++ b/solution.py
@@ -134,7 +134,8 @@
     send_rows = jnp.repeat(padded[slot_token].reshape(experts, capacity, width), PAIR, axis=0)
     arrived = lax.all_to_all(send_rows, "dev", split_axis=0, concat_axis=0, tiled=True)
     local_rows = arrived.reshape(-1, width)
-    piece = lax.all_gather(local_rows, "seq", axis=0, tiled=True)
+    sent = jnp.stack([local_rows] * lax.axis_size("seq"))
+    piece = jnp.concatenate(lax.all_to_all(sent, "seq", 0, 0), axis=0)
     gate_part = jnp.dot(piece, gate_weight[0], preferred_element_type=jnp.float32)
     up_part = jnp.dot(piece, up_weight[0], preferred_element_type=jnp.float32)
     hidden_all = (jax.nn.silu(gate_part) * up_part).astype(jnp.bfloat16)

time: 386 us -> 472 us (1.22)
  blocking collectives: 78.5 us -> 257 us
  waiting for transfers between devices: 231 us -> 132 us
  local copies, waits for them, and re-layouts: 8.93 us -> 18.8 us
    all_to_all x0 -> x1, blocking collectives: none -> 178 us  [per_device(): piece = jnp.concatenate(lax.all_to_all(sent, 'seq', 0, 0), axis=0)]
    all_gather x1 -> x0, waiting for transfers between devices: 95.2 us -> none  [per_device(): piece = lax.all_gather(local_rows, 'seq', axis=0, tiled=True)]
    another operation x0 -> x2, local copies, waits for them, and re-layouts: none -> 6.29 us  [per_device(): sent = jnp.stack([local_rows] * lax.axis_size('seq'))]
  transfers between devices with their start and end apart: 5 -> 4, of which waited for: 4 -> 3; matrix products, arithmetic and copies ran while one was open for 1% -> 1% of each run, Pallas kernels for 0% -> 0%
where the time goes in v1:
time: 472 us; the launch traced here: 471 us
  blocking collectives  257 us (54%)
  waiting for transfers between devices  132 us (28%)
  matrix products  27.3 us (6%)
  local copies, waits for them, and re-layouts  18.8 us (4%)
  starting transfers between devices  15.2 us (3%)
  between operations  14.3 us (3%)
  other arithmetic  6.12 us (1%)
    all_to_all x1, blocking collectives, per_device(): piece = jnp.concatenate(lax.all_to_all(sent, 'seq', 0, 0), axis=0)  178 us
    reduce_scatter x1, waiting for transfers between devices, per_device(): lax.psum_scatter(term.astype(jnp.float32).astype(jnp.bfloat16), 'seq', sc...  108 us
    unnamed x1, blocking collectives  62.8 us
    dot_general x1, matrix products, per_device(): jnp.dot(piece, down_weight[0], preferred_element_type=jnp.float32)  18.6 us
    all_to_all x1, waiting for transfers between devices, per_device(): lax.all_to_all(summed.reshape(dev_count, capacity, width).astype(jnp.bflo...  16.3 us
    all_to_all x1, blocking collectives, per_device(): lax.all_to_all(send_rows, 'dev', split_axis=0, concat_axis=0, tiled=True)  15.7 us
  transfers between devices with their start and end apart: 4, of which 3 were waited for; matrix products, arithmetic and copies ran while one was open for 1% of the time, Pallas kernels for 0%

profile of v1, /device:TPU:2, one launch (start us, length us, event | category | flops | bytes accessed | tf_op | source)
XLA Modules:
  0.0 471.1 jit_solution(11929414708672251249)
XLA Ops:
  6.5 0.0 copy-start
  6.5 0.0 all-gather.4.cloned.1.call-start
  6.5 1.0 reduce_window_sum.25
  7.5 0.2 slice_reduce_fusion
  7.7 0.1 exponential_bitcast_fusion.1
  7.8 2.0 convolution_convert_fusion.1
  9.8 0.0 all-gather.4.cloned.1.call-update
  9.8 1.3 dynamic-slice.8
  11.7 0.2 fusion.30
  11.9 0.2 dynamic-update-slice
  12.2 62.8 %all-reduce.1 = bf16[128]{0:T(256)(128)(2,1)S(1)} all-reduce(bf16[128]{0:T(256)(128)(2,1)S(1)} %dynamic-update-slice), channel_id=2, replica_groups=mesh['seq'=32,'dev'=8] {'seq'}, use_global_device_ids=true, to_apply=%add.1 | all-reduce | flops 128 | bytes 512
  75.0 0.1 reshape.265
  75.1 0.8 copy.29
  75.9 0.1 eq.27
  75.9 0.1 fusion.29
  76.0 0.7 broadcast_multiply_fusion
  76.7 0.1 copy.28
  76.8 0.1 mul.129
  76.9 0.2 select_reduce_fusion
  77.1 0.6 scatter_custom_fusion
  77.7 1.0 convolution_multiply_fusion.1
  78.8 0.0 all-gather.4.cloned.1.call-done
  78.8 2.1 while.3
  78.9 1.0 convert_add_fusion.2
  79.9 1.0 convert_add_fusion.2
  81.0 1.1 fusion.21
  82.1 1.1 fusion.13
  83.2 0.8 fusion.17
  84.1 0.1 copy.27
  84.1 0.7 all_to_all.23
  84.8 8.2 %all-to-all-start = ((bf16[8,8,512]{2,1,0:T(8,128)(2,1)}), bf16[8,8,512]{2,1,0:T(8,128)(2,1)S(1)}, u32[]{:S(2)}, u32[]{:S(2)}) async-start(bf16[8,8,512]{2,1,0:T(8,128)(2,1)} %all_to_all.23), calls=%async_computation | async-start | bytes 131072 | tf_op jit(solution)/shard_map/all_to_all | solution.py:127
  93.0 0.0 reduce-scatter.2.cloned.1.call-start
  93.0 8.3 %all-to-all-done = bf16[8,8,512]{2,1,0:T(8,128)(2,1)S(1)} async-done(((bf16[8,8,512]{2,1,0:T(8,128)(2,1)}), bf16[8,8,512]{2,1,0:T(8,128)(2,1)S(1)}, u32[]{:S(2)}, u32[]{:S(2)}) %all-to-all-start) | async-done | bytes 65568 | tf_op jit(solution)/shard_map/all_to_all | solution.py:127
  101.4 0.7 gather_fusion
  102.0 0.1 reshape.234
  102.2 15.7 %all_to_all.34 = bf16[8,6,4096]{2,1,0:T(8,128)(2,1)S(1)} all-to-all(bf16[8,6,4096]{2,1,0:T(8,128)(2,1)S(1)} %bitcast.117), channel_id=1, replica_groups=mesh['seq'=32,'dev'=8] {'dev'}, dimensions={0} | all-to-all | bytes 786432 | tf_op jit(solution)/shard_map/all_to_all | solution.py:135
  117.9 0.1 stack_reshape.2
  118.0 6.2 %stack.3 = bf16[32,48,4096]{2,1,0:T(8,128)(2,1)} broadcast(bf16[48,4096]{1,0:T(8,128)(2,1)S(1)} %stack_reshape.2), dimensions={1,2} | broadcast | bytes 12976128 | tf_op jit(solution)/shard_map/stack | solution.py:137
  124.1 0.0 copy-start.4
  124.2 178.4 %all_to_all.35 = bf16[32,48,4096]{2,1,0:T(8,128)(2,1)S(1)} all-to-all(bf16[32,48,4096]{2,1,0:T(8,128)(2,1)} %stack.3), channel_id=1, replica_groups=mesh['seq'=32,'dev'=8] {'seq'}, dimensions={0} | all-to-all | bytes 25165824 | tf_op jit(solution)/shard_map/all_to_all | solution.py:138
  302.5 0.0 copy-start.1
  302.5 0.0 copy-start.2
  302.5 4.5 copy-done.1
  307.0 0.0 copy-done.4
  307.0 3.4 fusion.4
  310.5 0.0 copy-done
  310.5 0.0 copy-done.2
  310.5 18.6 %convolution_convert_fusion = bf16[1536,4096]{1,0:T(8,128)(2,1)} fusion(bf16[1536,4096]{1,0:T(8,128)(2,1)} %bitcast.116, bf16[1,128,4096]{2,1,0:T(8,128)(2,1)S(1)} %copy-done, bf16[1,4096,128]{2,1,0:T(8,128)(2,1)S(1)} %copy-done.2, f32[1536,128]{1,0:T(8,128)S(1)} %fusion.4), kind=kOutput, calls=%fused_computation.5 | convolution fusion | flops 3228696576 | bytes 28049408 | tf_op jit(solution)/shard_map/dot_general | solution.py:143
  329.1 0.0 copy-start.3
  329.1 0.0 reduce-scatter.2.cloned.1.call-update
  329.1 107.7 %reduce-scatter.2.cloned.1.call-done = bf16[48,4096]{1,0:T(8,128)(2,1)} async-done(((bf16[1536,4096]{1,0:T(8,128)(2,1)}), bf16[48,4096]{1,0:T(8,128)(2,1)}) %reduce-scatter.2.cloned.1.call-update) | async-done | bytes 393232 | tf_op jit(solution)/shard_map/reduce_scatter | solution.py:145
  436.9 1.9 convert_element_type.99
  438.8 7.0 %all-to-all-start.3 = ((bf16[8,6,4096]{2,1,0:T(8,128)(2,1)}), bf16[8,6,4096]{2,1,0:T(8,128)(2,1)S(1)}, u32[]{:S(2)}, u32[]{:S(2)}) async-start(bf16[8,6,4096]{2,1,0:T(8,128)(2,1)} %convert_element_type.99), calls=%async_computation.4 | async-start | bytes 1048576 | tf_op jit(solution)/shard_map/all_to_all | solution.py:148
  445.8 0.0 copy-done.3
  445.8 0.1 copy.30
  445.9 16.3 %all-to-all-done.3 = bf16[8,6,4096]{2,1,0:T(8,128)(2,1)S(1)} async-done(((bf16[8,6,4096]{2,1,0:T(8,128)(2,1)}), bf16[8,6,4096]{2,1,0:T(8,128)(2,1)S(1)}, u32[]{:S(2)}, u32[]{:S(2)}) %all-to-all-start.3) | async-done | bytes 393248 | tf_op jit(solution)/shard_map/all_to_all | solution.py:148
  462.2 0.1 bitcast_reduce_fusion
  462.3 0.1 convert_element_type.101
  462.4 0.6 gather_fusion.1
  463.0 0.2 reshape.240
  463.2 1.0 multiply_reduce_fusion
  (14 shorter events, 0.2 us)
Async XLA Ops:
  6.5 303.9 %copy-start = (bf16[1,128,4096]{2,1,0:T(8,128)(2,1)S(1)}, bf16[1,128,4096]{2,1,0:T(8,128)(2,1)}, u32[]{:S(2)}) copy-start(bf16[1,128,4096]{2,1,0:T(8,128)(2,1)} %param.19) | copy-start | bytes 3145732
  6.5 72.3 %all-gather.4.cloned.1.call-start = ((), (), s32[]{:S(2)}) async-start(), calls=%async_computation.6 | async-start | bytes 4325376 | tf_op jit(solution)/shard_map/all_gather | solution.py:14
  84.8 16.6 %all-to-all-start = ((bf16[8,8,512]{2,1,0:T(8,128)(2,1)}), bf16[8,8,512]{2,1,0:T(8,128)(2,1)S(1)}, u32[]{:S(2)}, u32[]{:S(2)}) async-start(bf16[8,8,512]{2,1,0:T(8,128)(2,1)} %all_to_all.23), calls=%async_computation | async-start | bytes 131072 | tf_op jit(solution)/shard_map/all_to_all | solution.py:127
  93.0 343.9 %reduce-scatter.2.cloned.1.call-start = ((), (), s32[]{:S(2)}) async-start(), calls=%async_computation.5 | async-start | bytes 12976128 | tf_op jit(solution)/shard_map/reduce_scatter | solution.py:145
  124.1 182.9 %copy-start.4 = (bf16[1,4096,128]{2,1,0:T(8,128)(2,1)S(1)}, bf16[1,4096,128]{2,1,0:T(8,128)(2,1)}, u32[]{:S(2)}) copy-start(bf16[1,4096,128]{2,1,0:T(8,128)(2,1)} %param.17) | copy-start | bytes 3145732
  302.5 4.5 copy-start.1
  302.5 8.0 %copy-start.2 = (bf16[1,4096,128]{2,1,0:T(8,128)(2,1)S(1)}, bf16[1,4096,128]{2,1,0:T(8,128)(2,1)}, u32[]{:S(2)}) copy-start(bf16[1,4096,128]{2,1,0:T(8,128)(2,1)} %param.18) | copy-start | bytes 3145732
  329.1 116.7 %copy-start.3 = (f32[8,2]{0,1:T(2,128)S(1)}, f32[8,2]{0,1:T(2,128)}, u32[]{:S(2)}) copy-start(f32[8,2]{0,1:T(2,128)} %param.21) | copy-start | bytes 196
  438.8 23.4 %all-to-all-start.3 = ((bf16[8,6,4096]{2,1,0:T(8,128)(2,1)}), bf16[8,6,4096]{2,1,0:T(8,128)(2,1)S(1)}, u32[]{:S(2)}, u32[]{:S(2)}) async-start(bf16[8,6,4096]{2,1,0:T(8,128)(2,1)} %convert_element_type.99), calls=%async_computation.4 | async-start | bytes 1048576 | tf_op jit(solution)/shard_map/all_to_all | solution.py:148
Sparse Core Ops, SparseCore 0:
  9.9 53.7 all-gather.3
  329.3 107.5 reduce-scatter.1
